TPU v7x, 512 devices: a whole 4x8x8 slice. The times are simulated.
512 devices in a mesh: gx: 32 (over x, y), gy: 16 (over z, core).
Axes of the slice: x: 4, y: 8, z: 8, core: 2. Of those that a mesh axis runs over, the one named last changes fastest.
Arguments:
- right_side: bfloat16 [32, 16, 896, 128], P('gx', 'gy')
- schur_offdiag: bfloat16 [32, 16, 896, 896], P('gx', 'gy'), may hold values from -0.125 to 0.125
- schur_diag: float32 [32, 16, 896], P('gx', 'gy'), may hold values from 1.5 to 3
- trace_offdiag: bfloat16 [32, 16, 896, 896], P('gx', 'gy'), may hold values from -0.0390625 to 0.0390625
- trace_diag: float32 [32, 16, 896], P('gx', 'gy'), may hold values from 0.3 to 0.7
- couplings: bfloat16 [32, 16, 4, 128, 128], P('gx', 'gy'), may hold values from -0.375 to 0.375
- margin_rows: int32 [32, 16, 4, 128], P('gx', 'gy'), may hold values from 0 to 895, as said below
- deflation: bfloat16 [32, 16, 8, 896], P('gx', 'gy'), may hold values from -0.59765625 to 0.59765625
- coarse_inverse: float32 [4096, 4096], P(('gx', 'gy'))
- coarse_map: int32 [4096], replicated, may hold values from 0 to 4095, each once
Outputs:
- solution: float32 [32, 16, 896, 128], P('gx', 'gy')
- residual: float32 [32, 16, 896, 128], P('gx', 'gy')
Inputs may be any that keep to these rules, and one draw needn't show every extreme that they name: `margin_rows`: the 512 rows of one subdomain's four lists are all distinct. `coarse_map`: every coarse number appears once.
All inputs are finite; a program needn't handle non-finite values.
Results may differ from a plain program's by a relative error of at most 0.022.
Values may be sent and summed in bfloat16 or wider, within the bound.
No kernel may reach another device: no remote copies, remote signals or barrier semaphores. Data moves between devices by JAX's collectives and lax.ppermute only.
A program may use at most 64 MiB of HBM per device.

v0:
```python
import jax
import jax.numpy as jnp
from jax import lax
from jax.sharding import PartitionSpec as P

ITERS = 3


def from_behind(value, axis, steps):
    count = lax.axis_size(axis)
    leading, last = (max(0, -steps), min(count, count - steps))
    return lax.ppermute(value, axis, [(source, source + steps) for source in range(leading, last)])


def pass_columns(rows, offset):
    return from_behind(rows, "gx", offset)


def pass_lines(rows, offset):
    return from_behind(rows, "gy", offset)


def shards(
    right_side,
    schur_offdiag,
    schur_diag,
    trace_offdiag,
    trace_diag,
    couplings,
    margin_rows,
    deflation,
    coarse_inverse,
    coarse_map,
):
    rhs_wide = right_side[0, 0].astype(jnp.float32)
    schur_mat = schur_offdiag[0, 0]
    schur_scale = schur_diag[0, 0][:, None]
    trace_mat = trace_offdiag[0, 0]
    trace_scale = trace_diag[0, 0][:, None]
    coupling_blocks = couplings[0, 0]
    rows_lists = margin_rows[0, 0]
    flat_rows = rows_lists.reshape(-1)
    vectors = deflation[0, 0]
    vectors_wide = vectors.astype(jnp.float32).T
    coarse_cols = jnp.take(coarse_inverse, coarse_map, axis=1)

    def apply_schur(field):
        rounded = lax.optimization_barrier(field.astype(jnp.bfloat16))
        result = schur_scale * rounded.astype(jnp.float32) + jnp.dot(
            schur_mat, rounded, preferred_element_type=jnp.float32
        )
        sent_rows = rounded[rows_lists]
        received = jnp.stack(
            [
                pass_columns(sent_rows[1], 1),
                pass_columns(sent_rows[0], -1),
                pass_lines(sent_rows[3], 1),
                pass_lines(sent_rows[2], -1),
            ]
        )
        coupled = jnp.einsum(
            "dab,dbs->das", coupling_blocks, received, preferred_element_type=jnp.float32
        )
        return result.at[flat_rows].add(-coupled.reshape(-1, coupled.shape[-1]))

    def apply_prec(field):
        rounded = lax.optimization_barrier(field.astype(jnp.bfloat16))
        result = trace_scale * rounded.astype(jnp.float32) + jnp.dot(
            trace_mat, rounded, preferred_element_type=jnp.float32
        )
        coarse = jnp.dot(vectors, rounded, preferred_element_type=jnp.float32)
        stacked = lax.all_gather(coarse, ("gx", "gy"), axis=0, tiled=True)
        solved = jnp.dot(coarse_cols, stacked, precision=lax.Precision.HIGHEST)
        return result + jnp.dot(vectors_wide, solved, precision=lax.Precision.HIGHEST)

    solution = jnp.zeros(rhs_wide.shape, jnp.float32)
    direction = apply_prec(rhs_wide)
    for iteration in range(ITERS):
        image = apply_schur(direction)
        mapped = apply_prec(image)
        numer, denom = lax.psum(
            (jnp.sum(mapped * direction, axis=0), jnp.sum(mapped * mapped, axis=0)), ("gx", "gy")
        )
        alpha = numer / denom
        solution = solution + alpha * direction
        direction = direction - alpha * mapped
    residual = rhs_wide - apply_schur(solution)
    return (solution[None, None], residual[None, None])


def solution(mesh):
    return jax.shard_map(
        shards,
        mesh=mesh,
        in_specs=(
            P("gx", "gy", None, None),
            P("gx", "gy", None, None),
            P("gx", "gy", None),
            P("gx", "gy", None, None),
            P("gx", "gy", None),
            P("gx", "gy", None, None, None),
            P("gx", "gy", None, None),
            P("gx", "gy", None, None),
            P(("gx", "gy"), None),
            P(),
        ),
        out_specs=(P("gx", "gy", None, None), P("gx", "gy", None, None)),
        check_vma=False,
    )
```

profile of v0, /device:TPU:3, one launch (start us, length us, event | category | flops | bytes accessed | tf_op | source)
XLA Modules:
  0.0 902.4 jit_solution(9823042556222363306)
XLA Ops:
  12.1 15.7 %gather_fusion = f32[4096,8]{1,0:T(8,128)} fusion(f32[8,4096]{0,1:T(8,128)} %copy.24, s32[4096]{0:T(1024)S(1)} %fusion.131), kind=kCustom, calls=%fused_computation | custom fusion | bytes 278528 | tf_op jit(solution)/shard_map/jit(_take)/gather | solution.py:45
  27.8 105.3 %all-gather.5.cloned.1.call-done = f32[4096,128]{1,0:T(8,128)} async-done(((f32[8,128]{1,0:T(8,128)}), f32[4096,128]{1,0:T(8,128)}) %all-gather.5.cloned.1.call-update) | async-done | bytes 2097168 | tf_op jit(solution)/shard_map/all_gather | solution.py:72
  133.1 6.4 fusion.4
  144.1 3.1 collective-permute-start
  147.2 4.3 collective-permute-start.1
  151.5 3.4 collective-permute-start.2
  161.0 5.2 scatter_fusion
  168.2 111.2 %all-gather.7.cloned.1.call-done = f32[4096,128]{1,0:T(8,128)} async-done(((f32[8,128]{1,0:T(8,128)}), f32[4096,128]{1,0:T(8,128)}) %all-gather.7.cloned.1.call-update) | async-done | bytes 2097168 | tf_op jit(solution)/shard_map/all_gather | solution.py:72
  279.4 6.4 fusion.2
  287.7 95.9 %all-reduce.2 = (f32[128]{0:T(128)S(1)}, f32[128]{0:T(128)S(1)}) all-reduce(f32[128]{0:T(128)S(1)} %get-tuple-element.7, f32[128]{0:T(128)S(1)} %get-tuple-element.6), channel_id=1, replica_groups=mesh['gx'=32,'gy'=16] {'gx','gy'}, use_global_device_ids=true, to_apply=%region_2.3 | all-reduce | flops 256 | bytes 2048 | tf_op jit(solution)/shard_map/psum | solution.py:81
  390.2 5.5 collective-permute-start.5
  395.7 3.0 collective-permute-start.6
  404.8 5.2 scatter_fusion.1
  412.1 110.5 %all-gather.9.cloned.1.call-done = f32[4096,128]{1,0:T(8,128)} async-done(((f32[8,128]{1,0:T(8,128)}), f32[4096,128]{1,0:T(8,128)}) %all-gather.9.cloned.1.call-update) | async-done | bytes 2097168 | tf_op jit(solution)/shard_map/all_gather | solution.py:72
  522.5 6.4 fusion
  530.8 95.9 %all-reduce.1 = (f32[128]{0:T(128)S(1)}, f32[128]{0:T(128)S(1)}) all-reduce(f32[128]{0:T(128)S(1)} %get-tuple-element.5, f32[128]{0:T(128)S(1)} %get-tuple-element.4), channel_id=1, replica_groups=mesh['gx'=32,'gy'=16] {'gx','gy'}, use_global_device_ids=true, to_apply=%region_7.8 | all-reduce | flops 256 | bytes 2048 | tf_op jit(solution)/shard_map/psum | solution.py:81
  632.6 5.5 collective-permute-start.9
  647.2 5.2 scatter_fusion.2
  654.2 110.7 %all-gather.11.cloned.1.call-done = f32[4096,128]{1,0:T(8,128)} async-done(((f32[8,128]{1,0:T(8,128)}), f32[4096,128]{1,0:T(8,128)}) %all-gather.11.cloned.1.call-update) | async-done | bytes 2097168 | tf_op jit(solution)/shard_map/all_gather | solution.py:72
  764.9 6.4 fusion.6
  772.5 95.9 %all-reduce = (f32[128]{0:T(128)S(1)}, f32[128]{0:T(128)S(1)}) all-reduce(f32[128]{0:T(128)S(1)} %get-tuple-element.3, f32[128]{0:T(128)S(1)} %get-tuple-element.2), channel_id=1, replica_groups=mesh['gx'=32,'gy'=16] {'gx','gy'}, use_global_device_ids=true, to_apply=%region_12.13 | all-reduce | flops 256 | bytes 2048 | tf_op jit(solution)/shard_map/psum | solution.py:81
  875.3 5.5 collective-permute-start.13
  880.8 3.0 collective-permute-start.14
  889.2 4.8 scatter_fusion.3
  (112 shorter events, 68.0 us)
Async XLA Ops:
  7.2 132.8 %copy-start = (bf16[1,1,896,896]{3,2,1,0:T(8,128)(2,1)S(1)}, bf16[1,1,896,896]{3,2,1,0:T(8,128)(2,1)}, u32[]{:S(2)}) copy-start(bf16[1,1,896,896]{3,2,1,0:T(8,128)(2,1)} %param.13) | copy-start | bytes 4816900
  7.2 20.6 %copy-start.10 = (s32[1,1,4,128]{3,2,1,0:T(4,128)S(1)}, s32[1,1,4,128]{3,2,1,0:T(4,128)}, u32[]{:S(2)}) copy-start(s32[1,1,4,128]{3,2,1,0:T(4,128)} %param.16) | copy-start | bytes 6148
  7.2 125.9 %all-gather.5.cloned.1.call-start = ((), (), s32[]{:S(2)}) async-start(), calls=%async_computation | async-start | bytes 2101248 | tf_op jit(solution)/shard_map/all_gather | solution.py:72
  9.1 270.3 %all-gather.7.cloned.1.call-start = ((), (), s32[]{:S(2)}) async-start(), calls=%async_computation.1 | async-start | bytes 2101248 | tf_op jit(solution)/shard_map/all_gather | solution.py:72
  27.8 111.7 %copy-start.8 = (bf16[1,1,8,896]{3,2,1,0:T(8,128)(2,1)S(1)}, bf16[1,1,8,896]{3,2,1,0:T(8,128)(2,1)}, u32[]{:S(2)}) copy-start(bf16[1,1,8,896]{3,2,1,0:T(8,128)(2,1)} %param.17) | copy-start | bytes 43012
  143.3 16.9 %copy-start.13 = (bf16[1,1,4,128,128]{4,3,2,1,0:T(8,128)(2,1)S(1)}, bf16[1,1,4,128,128]{4,3,2,1,0:T(8,128)(2,1)}, u32[]{:S(2)}) copy-start(bf16[1,1,4,128,128]{4,3,2,1,0:T(8,128)(2,1)} %param.15) | copy-start | bytes 393220
  144.1 14.1 %collective-permute-start = (bf16[128,128]{1,0:T(8,128)(2,1)S(1)}, bf16[128,128]{1,0:T(8,128)(2,1)S(1)}, u32[]{:S(2)}, u32[]{:S(2)}) collective-permute-start(bf16[128,128]{1,0:T(8,128)(2,1)S(1)} %get-tuple-element.30), channel_id=1, source_target_pairs={{0,16},{16,32},{32,48},{48,64},{64,80},{80,96},{96,112},{112,128},... | collective-permute-start | bytes 98312 | tf_op jit(solution)/shard_map/ppermute | solution.py:12
  147.2 11.0 %collective-permute-start.1 = (bf16[128,128]{1,0:T(8,128)(2,1)S(1)}, bf16[128,128]{1,0:T(8,128)(2,1)S(1)}, u32[]{:S(2)}, u32[]{:S(2)}) collective-permute-start(bf16[128,128]{1,0:T(8,128)(2,1)S(1)} %get-tuple-element.32), channel_id=1, source_target_pairs={{16,0},{32,16},{48,32},{64,48},{80,64},{96,80},{112,96},{128,112},... | collective-permute-start | bytes 98312 | tf_op jit(solution)/shard_map/ppermute | solution.py:12
  151.5 6.7 collective-permute-start.2
  154.9 5.2 collective-permute-start.3
  168.0 354.6 %all-gather.9.cloned.1.call-start = ((), (), s32[]{:S(2)}) async-start(), calls=%async_computation.2 | async-start | bytes 2101248 | tf_op jit(solution)/shard_map/all_gather | solution.py:72
  388.3 13.7 %collective-permute-start.4 = (bf16[128,128]{1,0:T(8,128)(2,1)S(1)}, bf16[128,128]{1,0:T(8,128)(2,1)S(1)}, u32[]{:S(2)}, u32[]{:S(2)}) collective-permute-start(bf16[128,128]{1,0:T(8,128)(2,1)S(1)} %get-tuple-element.26), channel_id=1, source_target_pairs={{0,16},{16,32},{32,48},{48,64},{64,80},{80,96},{96,112},{112,128},... | collective-permute-start | bytes 98312 | tf_op jit(solution)/shard_map/ppermute | solution.py:12
  390.2 11.8 %collective-permute-start.5 = (bf16[128,128]{1,0:T(8,128)(2,1)S(1)}, bf16[128,128]{1,0:T(8,128)(2,1)S(1)}, u32[]{:S(2)}, u32[]{:S(2)}) collective-permute-start(bf16[128,128]{1,0:T(8,128)(2,1)S(1)} %get-tuple-element.28), channel_id=1, source_target_pairs={{16,0},{32,16},{48,32},{64,48},{80,64},{96,80},{112,96},{128,112},... | collective-permute-start | bytes 98312 | tf_op jit(solution)/shard_map/ppermute | solution.py:12
  395.7 6.3 collective-permute-start.6
  398.7 5.2 collective-permute-start.7
  411.8 353.1 %all-gather.11.cloned.1.call-start = ((), (), s32[]{:S(2)}) async-start(), calls=%async_computation.3 | async-start | bytes 2101248 | tf_op jit(solution)/shard_map/all_gather | solution.py:72
  630.7 13.7 %collective-permute-start.8 = (bf16[128,128]{1,0:T(8,128)(2,1)S(1)}, bf16[128,128]{1,0:T(8,128)(2,1)S(1)}, u32[]{:S(2)}, u32[]{:S(2)}) collective-permute-start(bf16[128,128]{1,0:T(8,128)(2,1)S(1)} %get-tuple-element.22), channel_id=1, source_target_pairs={{0,16},{16,32},{32,48},{48,64},{64,80},{80,96},{96,112},{112,128},... | collective-permute-start | bytes 98312 | tf_op jit(solution)/shard_map/ppermute | solution.py:12
  632.6 11.8 %collective-permute-start.9 = (bf16[128,128]{1,0:T(8,128)(2,1)S(1)}, bf16[128,128]{1,0:T(8,128)(2,1)S(1)}, u32[]{:S(2)}, u32[]{:S(2)}) collective-permute-start(bf16[128,128]{1,0:T(8,128)(2,1)S(1)} %get-tuple-element.24), channel_id=1, source_target_pairs={{16,0},{32,16},{48,32},{64,48},{80,64},{96,80},{112,96},{128,112},... | collective-permute-start | bytes 98312 | tf_op jit(solution)/shard_map/ppermute | solution.py:12
  638.1 6.3 collective-permute-start.10
  641.1 5.2 collective-permute-start.11
  873.4 13.7 %collective-permute-start.12 = (bf16[128,128]{1,0:T(8,128)(2,1)S(1)}, bf16[128,128]{1,0:T(8,128)(2,1)S(1)}, u32[]{:S(2)}, u32[]{:S(2)}) collective-permute-start(bf16[128,128]{1,0:T(8,128)(2,1)S(1)} %get-tuple-element.18), channel_id=1, source_target_pairs={{0,16},{16,32},{32,48},{48,64},{64,80},{80,96},{96,112},{112,128},... | collective-permute-start | bytes 98312 | tf_op jit(solution)/shard_map/ppermute | solution.py:12
  875.3 11.8 %collective-permute-start.13 = (bf16[128,128]{1,0:T(8,128)(2,1)S(1)}, bf16[128,128]{1,0:T(8,128)(2,1)S(1)}, u32[]{:S(2)}, u32[]{:S(2)}) collective-permute-start(bf16[128,128]{1,0:T(8,128)(2,1)S(1)} %get-tuple-element.20), channel_id=1, source_target_pairs={{16,0},{32,16},{48,32},{64,48},{80,64},{96,80},{112,96},{128,112},... | collective-permute-start | bytes 98312 | tf_op jit(solution)/shard_map/ppermute | solution.py:12
  880.8 6.3 collective-permute-start.14
  883.8 5.2 collective-permute-start.15
  (13 other events, 120.1 us)
Sparse Core Ops, SparseCore 0:
  12.8 120.2 all-gather.4
  168.1 111.2 all-gather.6
  411.9 110.5 all-gather.8
  654.3 110.5 all-gather.10
where the time goes:
time: 904 us; the launch traced here: 902 us
  waiting for transfers between devices  445 us (49%)
  blocking collectives  288 us (32%)
  starting transfers between devices  50.2 us (6%)
  matrix products  44.5 us (5%)
  other arithmetic  30.7 us (3%)
  local copies, waits for them, and re-layouts  29.7 us (3%)
  between operations  14.2 us (2%)
    all_gather x4, waiting for transfers between devices, apply_prec(): stacked = lax.all_gather(coarse, ('gx', 'gy'), axis=0, tiled=True)  438 us
    psum x3, blocking collectives, shards(): lax.psum((jnp.sum(mapped * direction, axis=0), jnp.sum(mapped * mapped, a...  288 us
    ppermute x16, starting transfers between devices, from_behind(): lax.ppermute(value, axis, [(source, source + steps) for source in range(l...  49.6 us
    dot_general x4, matrix products, apply_prec(): solved = jnp.dot(coarse_cols, stacked, precision=lax.Precision.HIGHEST)  25.7 us
    scatter-add x4, other arithmetic, apply_schur(): return result.at[flat_rows].add(-coupled.reshape(-1, coupled.shape[-1]))  20.3 us
  transfers between devices with their start and end apart: 20, of which 8 were waited for; matrix products, arithmetic and copies ran while one was open for 3% of the time, Pallas kernels for 0%

commit v1 on v0

--- a/solution.py
+++ b/solution.py
@@ -1,9 +1,19 @@
+import functools
 import jax
 import jax.numpy as jnp
 from jax import lax
 from jax.sharding import PartitionSpec as P
 
 ITERS = 3
+
+
+def detail_floor(m, peer_axis):
+    return jnp.concatenate(
+        lax.all_to_all(jnp.stack([m] * lax.axis_size(peer_axis)), peer_axis, 0, 0), axis=0
+    )
+
+
+_note_regions = functools.partial(detail_floor, peer_axis=("gx", "gy"))
 
 
 def from_behind(value, axis, steps):
@@ -69,7 +79,7 @@
             trace_mat, rounded, preferred_element_type=jnp.float32
         )
         coarse = jnp.dot(vectors, rounded, preferred_element_type=jnp.float32)
-        stacked = lax.all_gather(coarse, ("gx", "gy"), axis=0, tiled=True)
+        stacked = _note_regions(coarse)
         solved = jnp.dot(coarse_cols, stacked, precision=lax.Precision.HIGHEST)
         return result + jnp.dot(vectors_wide, solved, precision=lax.Precision.HIGHEST)
 

time: 904 us -> 702 us (0.78)
  waiting for transfers between devices: 445 us -> 40.6 us
  blocking collectives: 288 us -> 478 us
  starting transfers between devices: 50.2 us -> 75.7 us
  between operations: 14.2 us -> 1.31 us
    all_gather x4 -> x0, waiting for transfers between devices: 438 us -> none  [apply_prec(): stacked = lax.all_gather(coarse, ('gx', 'gy'), axis=0, tiled=True)]
    all_to_all x0 -> x3, blocking collectives: none -> 189 us  [detail_floor(): lax.all_to_all(jnp.stack([m] * lax.axis_size(peer_axis)), peer_axis, 0, 0)]
    all_to_all x0 -> x1, waiting for transfers between devices: none -> 32.9 us  [detail_floor(): lax.all_to_all(jnp.stack([m] * lax.axis_size(peer_axis)), peer_axis, 0, 0)]
    all_to_all x0 -> x1, starting transfers between devices: none -> 23.6 us  [detail_floor(): lax.all_to_all(jnp.stack([m] * lax.axis_size(peer_axis)), peer_axis, 0, 0)]
  transfers between devices with their start and end apart: 20 -> 17, of which waited for: 8 -> 5; matrix products, arithmetic and copies ran while one was open for 3% -> 3% of each run, Pallas kernels for 0% -> 0%
where the time goes in v1:
time: 702 us; the launch traced here: 692 us
  blocking collectives  478 us (68%)
  starting transfers between devices  75.7 us (11%)
  waiting for transfers between devices  40.6 us (6%)
  matrix products  35.7 us (5%)
  local copies, waits for them, and re-layouts  30.7 us (4%)
  other arithmetic  30.7 us (4%)
    psum x3, blocking collectives, shards(): lax.psum((jnp.sum(mapped * direction, axis=0), jnp.sum(mapped * mapped, a...  288 us
    all_to_all x3, blocking collectives, detail_floor(): lax.all_to_all(jnp.stack([m] * lax.axis_size(peer_axis)), peer_axis, 0, 0)  189 us
    ppermute x16, starting transfers between devices, from_behind(): lax.ppermute(value, axis, [(source, source + steps) for source in range(l...  52.1 us
    all_to_all x1, waiting for transfers between devices, detail_floor(): lax.all_to_all(jnp.stack([m] * lax.axis_size(peer_axis)), peer_axis, 0, 0)  32.9 us
    all_to_all x1, starting transfers between devices, detail_floor(): lax.all_to_all(jnp.stack([m] * lax.axis_size(peer_axis)), peer_axis, 0, 0)  23.6 us
    scatter-add x4, other arithmetic, apply_schur(): return result.at[flat_rows].add(-coupled.reshape(-1, coupled.shape[-1]))  20.3 us
    dot_general x4, matrix products, apply_prec(): solved = jnp.dot(coarse_cols, stacked, precision=lax.Precision.HIGHEST)  19.2 us
    gather x1, local copies, waits for them, and re-layouts, shards(): coarse_cols = jnp.take(coarse_inverse, coarse_map, axis=1)  15.7 us
  transfers between devices with their start and end apart: 17, of which 5 were waited for; matrix products, arithmetic and copies ran while one was open for 3% of the time, Pallas kernels for 0%

profile of v1, /device:TPU:3, one launch (start us, length us, event | category | flops | bytes accessed | tf_op | source)
XLA Modules:
  0.0 692.4 jit_solution(16561879557193525579)
XLA Ops:
  3.3 23.6 %all-to-all-start = ((f32[512,8,128]{2,1,0:T(8,128)}), f32[512,8,128]{2,1,0:T(8,128)}, u32[]{:S(2)}, u32[]{:S(2)}) async-start(f32[512,8,128]{2,1,0:T(8,128)} %stack.48), calls=%async_computation | async-start | bytes 4194304 | tf_op jit(solution)/shard_map/all_to_all | solution.py:12
  29.0 15.7 %gather_fusion = f32[4096,8]{1,0:T(8,128)} fusion(f32[8,4096]{0,1:T(8,128)} %copy.12, s32[4096]{0:T(1024)S(1)} %fusion.135), kind=kCustom, calls=%fused_computation | custom fusion | bytes 278528 | tf_op jit(solution)/shard_map/jit(_take)/gather | solution.py:55
  44.7 32.9 %all-to-all-done = f32[512,8,128]{2,1,0:T(8,128)} async-done(((f32[512,8,128]{2,1,0:T(8,128)}), f32[512,8,128]{2,1,0:T(8,128)}, u32[]{:S(2)}, u32[]{:S(2)}) %all-to-all-start) | async-done | bytes 2097184 | tf_op jit(solution)/shard_map/all_to_all | solution.py:12
  77.6 6.4 fusion.6
  88.6 3.8 collective-permute-start
  95.1 5.1 collective-permute-start.1
  106.4 5.2 scatter_fusion
  112.9 62.0 %all_to_all.20 = f32[512,8,128]{2,1,0:T(8,128)S(1)} all-to-all(f32[512,8,128]{2,1,0:T(8,128)S(1)} %stack.54), channel_id=1, replica_groups=mesh['gx'=32,'gy'=16] {'gx','gy'}, dimensions={0} | all-to-all | bytes 4194304 | tf_op jit(solution)/shard_map/all_to_all | solution.py:12
  174.9 4.3 fusion.4
  181.0 96.1 %all-reduce.2 = (f32[128]{0:T(128)S(1)}, f32[128]{0:T(128)S(1)}) all-reduce(f32[128]{0:T(128)S(1)} %get-tuple-element.7, f32[128]{0:T(128)S(1)} %get-tuple-element.6), channel_id=1, replica_groups=mesh['gx'=32,'gy'=16] {'gx','gy'}, use_global_device_ids=true, to_apply=%region_2.3 | all-reduce | flops 256 | bytes 2048 | tf_op jit(solution)/shard_map/psum | solution.py:91
  284.4 2.9 collective-permute-start.6
  287.3 5.4 collective-permute-start.5
  298.9 5.2 scatter_fusion.1
  305.4 63.7 %all_to_all.21 = f32[512,8,128]{2,1,0:T(8,128)S(1)} all-to-all(f32[512,8,128]{2,1,0:T(8,128)S(1)} %stack.60), channel_id=1, replica_groups=mesh['gx'=32,'gy'=16] {'gx','gy'}, dimensions={0} | all-to-all | bytes 4194304 | tf_op jit(solution)/shard_map/all_to_all | solution.py:12
  369.1 4.3 fusion.2
  375.2 96.1 %all-reduce.1 = (f32[128]{0:T(128)S(1)}, f32[128]{0:T(128)S(1)}) all-reduce(f32[128]{0:T(128)S(1)} %get-tuple-element.5, f32[128]{0:T(128)S(1)} %get-tuple-element.4), channel_id=1, replica_groups=mesh['gx'=32,'gy'=16] {'gx','gy'}, use_global_device_ids=true, to_apply=%region_7.8 | all-reduce | flops 256 | bytes 2048 | tf_op jit(solution)/shard_map/psum | solution.py:91
  477.9 2.9 collective-permute-start.10
  480.8 5.4 collective-permute-start.9
  492.4 5.2 scatter_fusion.2
  498.9 63.7 %all_to_all.22 = f32[512,8,128]{2,1,0:T(8,128)S(1)} all-to-all(f32[512,8,128]{2,1,0:T(8,128)S(1)} %stack.66), channel_id=1, replica_groups=mesh['gx'=32,'gy'=16] {'gx','gy'}, dimensions={0} | all-to-all | bytes 4194304 | tf_op jit(solution)/shard_map/all_to_all | solution.py:12
  562.6 4.3 fusion
  568.0 96.1 %all-reduce = (f32[128]{0:T(128)S(1)}, f32[128]{0:T(128)S(1)}) all-reduce(f32[128]{0:T(128)S(1)} %get-tuple-element.3, f32[128]{0:T(128)S(1)} %get-tuple-element.2), channel_id=1, replica_groups=mesh['gx'=32,'gy'=16] {'gx','gy'}, use_global_device_ids=true, to_apply=%region_12.13 | all-reduce | flops 256 | bytes 2048 | tf_op jit(solution)/shard_map/psum | solution.py:91
  674.6 5.4 collective-permute-start.13
  685.5 4.8 scatter_fusion.3
  (117 shorter events, 70.8 us)
Async XLA Ops:
  0.6 83.9 %copy-start = (bf16[1,1,896,896]{3,2,1,0:T(8,128)(2,1)S(1)}, bf16[1,1,896,896]{3,2,1,0:T(8,128)(2,1)}, u32[]{:S(2)}) copy-start(bf16[1,1,896,896]{3,2,1,0:T(8,128)(2,1)} %param.13) | copy-start | bytes 4816900
  3.3 23.7 %copy-start.16 = (f32[1,1,896]{2,1,0:T(1,128)S(1)}, f32[1,1,896]{2,1,0:T(1,128)}, u32[]{:S(2)}) copy-start(f32[1,1,896]{2,1,0:T(1,128)} %param.14) | copy-start | bytes 10756
  3.3 23.7 %copy-start.12 = (f32[8,4096]{1,0:T(8,128)S(1)}, f32[8,4096]{1,0:T(8,128)}, u32[]{:S(2)}) copy-start(f32[8,4096]{1,0:T(8,128)} %param.18) | copy-start | bytes 393220
  3.3 74.3 %all-to-all-start = ((f32[512,8,128]{2,1,0:T(8,128)}), f32[512,8,128]{2,1,0:T(8,128)}, u32[]{:S(2)}, u32[]{:S(2)}) async-start(f32[512,8,128]{2,1,0:T(8,128)} %stack.48), calls=%async_computation | async-start | bytes 4194304 | tf_op jit(solution)/shard_map/all_to_all | solution.py:12
  44.7 39.3 %copy-start.11 = (bf16[1,1,8,896]{3,2,1,0:T(8,128)(2,1)S(1)}, bf16[1,1,8,896]{3,2,1,0:T(8,128)(2,1)}, u32[]{:S(2)}) copy-start(bf16[1,1,8,896]{3,2,1,0:T(8,128)(2,1)} %param.17) | copy-start | bytes 43012
  88.6 14.9 %collective-permute-start = (bf16[128,128]{1,0:T(8,128)(2,1)S(1)}, bf16[128,128]{1,0:T(8,128)(2,1)S(1)}, u32[]{:S(2)}, u32[]{:S(2)}) collective-permute-start(bf16[128,128]{1,0:T(8,128)(2,1)S(1)} %get-tuple-element.30), channel_id=1, source_target_pairs={{0,16},{16,32},{32,48},{48,64},{64,80},{80,96},{96,112},{112,128},... | collective-permute-start | bytes 98312 | tf_op jit(solution)/shard_map/ppermute | solution.py:22
  92.4 11.2 %collective-permute-start.2 = (bf16[128,128]{1,0:T(8,128)(2,1)S(1)}, bf16[128,128]{1,0:T(8,128)(2,1)S(1)}, u32[]{:S(2)}, u32[]{:S(2)}) collective-permute-start(bf16[128,128]{1,0:T(8,128)(2,1)S(1)} %get-tuple-element.31), channel_id=1, source_target_pairs={{0,1},{1,2},{2,3},{3,4},{4,5},{5,6},{6,7},{7,8},{8,9},{9,10},{10,1... | collective-permute-start | bytes 98312 | tf_op jit(solution)/shard_map/ppermute | solution.py:22
  95.1 8.5 %collective-permute-start.1 = (bf16[128,128]{1,0:T(8,128)(2,1)S(1)}, bf16[128,128]{1,0:T(8,128)(2,1)S(1)}, u32[]{:S(2)}, u32[]{:S(2)}) collective-permute-start(bf16[128,128]{1,0:T(8,128)(2,1)S(1)} %get-tuple-element.32), channel_id=1, source_target_pairs={{16,0},{32,16},{48,32},{64,48},{80,64},{96,80},{112,96},{128,112},... | collective-permute-start | bytes 98312 | tf_op jit(solution)/shard_map/ppermute | solution.py:22
  100.3 5.2 collective-permute-start.3
  112.9 62.0 %copy-start.1 = (f32[4096,8]{1,0:T(8,128)S(1)}, f32[4096,8]{1,0:T(8,128)}, u32[]{:S(2)}) copy-start(f32[4096,8]{1,0:T(8,128)} %gather_fusion) | copy-start | bytes 393220
  281.8 14.3 %collective-permute-start.4 = (bf16[128,128]{1,0:T(8,128)(2,1)S(1)}, bf16[128,128]{1,0:T(8,128)(2,1)S(1)}, u32[]{:S(2)}, u32[]{:S(2)}) collective-permute-start(bf16[128,128]{1,0:T(8,128)(2,1)S(1)} %get-tuple-element.26), channel_id=1, source_target_pairs={{0,16},{16,32},{32,48},{48,64},{64,80},{80,96},{96,112},{112,128},... | collective-permute-start | bytes 98312 | tf_op jit(solution)/shard_map/ppermute | solution.py:22
  284.4 11.6 %collective-permute-start.6 = (bf16[128,128]{1,0:T(8,128)(2,1)S(1)}, bf16[128,128]{1,0:T(8,128)(2,1)S(1)}, u32[]{:S(2)}, u32[]{:S(2)}) collective-permute-start(bf16[128,128]{1,0:T(8,128)(2,1)S(1)} %get-tuple-element.27), channel_id=1, source_target_pairs={{0,1},{1,2},{2,3},{3,4},{4,5},{5,6},{6,7},{7,8},{8,9},{9,10},{10,1... | collective-permute-start | bytes 98312 | tf_op jit(solution)/shard_map/ppermute | solution.py:22
  287.3 8.7 %collective-permute-start.5 = (bf16[128,128]{1,0:T(8,128)(2,1)S(1)}, bf16[128,128]{1,0:T(8,128)(2,1)S(1)}, u32[]{:S(2)}, u32[]{:S(2)}) collective-permute-start(bf16[128,128]{1,0:T(8,128)(2,1)S(1)} %get-tuple-element.28), channel_id=1, source_target_pairs={{16,0},{32,16},{48,32},{64,48},{80,64},{96,80},{112,96},{128,112},... | collective-permute-start | bytes 98312 | tf_op jit(solution)/shard_map/ppermute | solution.py:22
  292.8 5.2 collective-permute-start.7
  305.4 63.7 %copy-start.2 = (f32[4096,8]{1,0:T(8,128)S(1)}, f32[4096,8]{1,0:T(8,128)}, u32[]{:S(2)}) copy-start(f32[4096,8]{1,0:T(8,128)} %gather_fusion) | copy-start | bytes 393220
  475.3 14.3 %collective-permute-start.8 = (bf16[128,128]{1,0:T(8,128)(2,1)S(1)}, bf16[128,128]{1,0:T(8,128)(2,1)S(1)}, u32[]{:S(2)}, u32[]{:S(2)}) collective-permute-start(bf16[128,128]{1,0:T(8,128)(2,1)S(1)} %get-tuple-element.22), channel_id=1, source_target_pairs={{0,16},{16,32},{32,48},{48,64},{64,80},{80,96},{96,112},{112,128},... | collective-permute-start | bytes 98312 | tf_op jit(solution)/shard_map/ppermute | solution.py:22
  477.9 11.6 %collective-permute-start.10 = (bf16[128,128]{1,0:T(8,128)(2,1)S(1)}, bf16[128,128]{1,0:T(8,128)(2,1)S(1)}, u32[]{:S(2)}, u32[]{:S(2)}) collective-permute-start(bf16[128,128]{1,0:T(8,128)(2,1)S(1)} %get-tuple-element.23), channel_id=1, source_target_pairs={{0,1},{1,2},{2,3},{3,4},{4,5},{5,6},{6,7},{7,8},{8,9},{9,10},{10,1... | collective-permute-start | bytes 98312 | tf_op jit(solution)/shard_map/ppermute | solution.py:22
  480.8 8.7 %collective-permute-start.9 = (bf16[128,128]{1,0:T(8,128)(2,1)S(1)}, bf16[128,128]{1,0:T(8,128)(2,1)S(1)}, u32[]{:S(2)}, u32[]{:S(2)}) collective-permute-start(bf16[128,128]{1,0:T(8,128)(2,1)S(1)} %get-tuple-element.24), channel_id=1, source_target_pairs={{16,0},{32,16},{48,32},{64,48},{80,64},{96,80},{112,96},{128,112},... | collective-permute-start | bytes 98312 | tf_op jit(solution)/shard_map/ppermute | solution.py:22
  486.2 5.2 collective-permute-start.11
  498.9 63.7 %copy-start.3 = (f32[4096,8]{1,0:T(8,128)S(1)}, f32[4096,8]{1,0:T(8,128)}, u32[]{:S(2)}) copy-start(f32[4096,8]{1,0:T(8,128)} %gather_fusion) | copy-start | bytes 393220
  669.1 14.3 %collective-permute-start.12 = (bf16[128,128]{1,0:T(8,128)(2,1)S(1)}, bf16[128,128]{1,0:T(8,128)(2,1)S(1)}, u32[]{:S(2)}, u32[]{:S(2)}) collective-permute-start(bf16[128,128]{1,0:T(8,128)(2,1)S(1)} %get-tuple-element.18), channel_id=1, source_target_pairs={{0,16},{16,32},{32,48},{48,64},{64,80},{80,96},{96,112},{112,128},... | collective-permute-start | bytes 98312 | tf_op jit(solution)/shard_map/ppermute | solution.py:22
  671.7 11.6 %collective-permute-start.14 = (bf16[128,128]{1,0:T(8,128)(2,1)S(1)}, bf16[128,128]{1,0:T(8,128)(2,1)S(1)}, u32[]{:S(2)}, u32[]{:S(2)}) collective-permute-start(bf16[128,128]{1,0:T(8,128)(2,1)S(1)} %get-tuple-element.19), channel_id=1, source_target_pairs={{0,1},{1,2},{2,3},{3,4},{4,5},{5,6},{6,7},{7,8},{8,9},{9,10},{10,1... | collective-permute-start | bytes 98312 | tf_op jit(solution)/shard_map/ppermute | solution.py:22
  674.6 8.7 %collective-permute-start.13 = (bf16[128,128]{1,0:T(8,128)(2,1)S(1)}, bf16[128,128]{1,0:T(8,128)(2,1)S(1)}, u32[]{:S(2)}, u32[]{:S(2)}) collective-permute-start(bf16[128,128]{1,0:T(8,128)(2,1)S(1)} %get-tuple-element.20), channel_id=1, source_target_pairs={{16,0},{32,16},{48,32},{64,48},{80,64},{96,80},{112,96},{128,112},... | collective-permute-start | bytes 98312 | tf_op jit(solution)/shard_map/ppermute | solution.py:22
  680.1 5.2 collective-permute-start.15
  (14 other events, 160.6 us)
